TPU v7x, 128 devices: a whole 4x4x4 slice. The times are simulated.
128 devices in a mesh: leaf: 16 (over y, z), ctx: 8 (over x, core).
Axes of the slice: x: 4, y: 4, z: 4, core: 2. Of those that a mesh axis runs over, the one named last changes fastest.
Arguments:
- query_key_value_rows: bfloat16 [16384, 7168], P(('leaf', 'ctx')), may hold values from -6 to 6
- cotangent: bfloat16 [16384, 5120], P(('leaf', 'ctx')), may hold values from -6 to 6
- out_weight: bfloat16 [5120, 5120], P('ctx'), may hold values from -0.078125 to 0.078125
- parents: int32 [16, 8], P('leaf'), may hold values from 0 to 6, as said below
- rollout_spans: int32 [16384], P('leaf'), may hold values from 64 to 4096
Outputs:
- qkv_grad: bfloat16 [16384, 7168], P(('leaf', 'ctx'))
- weight_grad: bfloat16 [5120, 5120], P('ctx')
Inputs may be any that keep to these rules, and one draw needn't show every extreme that they name: parents[t, 0] = 0, every later block's parent is an earlier block of the same tree, and the last block's parent is the block just before it.
All inputs are finite; a program needn't handle non-finite values.
Results may differ from a plain program's by a relative error of at most 0.012.
The roundings to bfloat16 on the way count: a program that leaves them out, or rounds other values in their place, can miss the bound.
Values may be sent and summed in bfloat16 or wider, within the bound.
No kernel may reach another device: no remote copies, remote signals or barrier semaphores. Data moves between devices by JAX's collectives and lax.ppermute only.
A program may use at most 192 MiB of HBM per device.

v0:
```python
import math
import jax
import jax.numpy as jnp
from jax import lax
from jax.sharding import PartitionSpec as P

QUERY_HEADS = 40
KEY_VALUE_HEADS = 8
HEAD_SIZE = 128
BLK = 128
log_base = 1024.0


def ancestors(parents):
    number = parents.shape[0]
    indices = jnp.arange(number, dtype=jnp.int32)

    def advance(iteration, state):
        current, reached = state
        current = jnp.sum(
            jnp.where(current[:, None] == indices[None, :], parents[None, :], 0), axis=1
        )
        return (current, reached | (current[:, None] == indices[None, :]))

    return lax.fori_loop(0, number, advance, (indices, indices[:, None] == indices[None, :]))[1]


def token_mask(reached, first_row, query_count, key_count):
    query_pos = first_row + jnp.arange(query_count, dtype=jnp.int32)
    key_pos = jnp.arange(key_count, dtype=jnp.int32)
    block_part = reached[first_row // BLK : (first_row + query_count) // BLK, : key_count // BLK]
    expanded = jnp.repeat(jnp.repeat(block_part, BLK, axis=0), BLK, axis=1)
    same_block = (query_pos // BLK)[:, None] == (key_pos // BLK)[None, :]
    return expanded & (jnp.logical_not(same_block) | (key_pos[None, :] <= query_pos[:, None]))


def span_softness(rollout_spans):
    return jnp.log(rollout_spans.astype(jnp.float32)) * (
        1.0 / (math.log(log_base) * math.sqrt(HEAD_SIZE))
    )


def contract_rows(left, right):
    return lax.dot_general(
        left, right, (((0,), (0,)), ((), ())), preferred_element_type=jnp.float32
    )


def contract_cols(left, right):
    return lax.dot_general(
        left, right, (((1,), (1,)), ((), ())), preferred_element_type=jnp.float32
    )


def local(query_key_value_rows, cotangent, out_weight, parents, rollout_spans):
    queries_per_group = QUERY_HEADS // KEY_VALUE_HEADS
    head_rows = lax.all_to_all(query_key_value_rows, "ctx", split_axis=1, concat_axis=0, tiled=True)
    tree_len = head_rows.shape[0]
    kv_local = head_rows.shape[1] // ((queries_per_group + 2) * HEAD_SIZE)
    heads_local = kv_local * queries_per_group
    grouped = head_rows.reshape(tree_len, kv_local, queries_per_group + 2, HEAD_SIZE)
    asking_matrix = grouped[:, :, :queries_per_group]
    lookup_matrix = grouped[:, :, queries_per_group]
    value_rows = grouped[:, :, queries_per_group + 1]
    softness_multiplier = span_softness(rollout_spans)
    reached = ancestors(parents[0])
    block_len = min(512, tree_len)
    block_total = tree_len // block_len
    masks = []
    total_parts = []
    attended_parts = []
    for block_id in range(block_total):
        opening_slot = block_id * block_len
        closing_slot = opening_slot + block_len
        allowed = token_mask(reached, opening_slot, block_len, closing_slot)
        masks.append(allowed)
        attention_logits = jnp.einsum(
            "zpyr,kpr->pyzk",
            asking_matrix[opening_slot:closing_slot],
            lookup_matrix[:closing_slot],
            preferred_element_type=jnp.float32,
        )
        attention_logits = jnp.where(
            allowed[None, None],
            attention_logits * softness_multiplier[opening_slot:closing_slot][None, None, :, None],
            -jnp.inf,
        )
        peak_score = jnp.max(attention_logits, axis=-1, keepdims=True)
        log_total = peak_score + jnp.log(
            jnp.sum(jnp.exp(attention_logits - peak_score), axis=-1, keepdims=True)
        )
        weights_low = jnp.exp(attention_logits - log_total).astype(jnp.bfloat16)
        attended_parts.append(
            jnp.einsum(
                "gjts,sgd->tgjd",
                weights_low,
                value_rows[:closing_slot],
                preferred_element_type=jnp.float32,
            ).astype(jnp.bfloat16)
        )
        total_parts.append(log_total[..., 0])
    attended = jnp.concatenate(attended_parts, axis=0)
    log_totals = jnp.concatenate(total_parts, axis=2)
    flat_out = attended.reshape(tree_len, heads_local * HEAD_SIZE)
    shard_rows = lax.all_gather(cotangent, "ctx", axis=0, tiled=True)
    weight_low = contract_rows(flat_out, shard_rows).astype(jnp.bfloat16)
    asking_heads = jnp.transpose(asking_matrix.reshape(tree_len, heads_local, HEAD_SIZE), (1, 0, 2))
    attended_heads = jnp.transpose(attended.reshape(tree_len, heads_local, HEAD_SIZE), (1, 0, 2))
    (
        weight_low,
        shard_rows,
        masks,
        asking_heads,
        attended_heads,
        lookup_matrix,
        value_rows,
        log_totals,
    ) = lax.optimization_barrier(
        (
            weight_low,
            shard_rows,
            masks,
            asking_heads,
            attended_heads,
            lookup_matrix,
            value_rows,
            log_totals,
        )
    )
    weight_total = lax.psum(weight_low, "leaf")

    def backward_part():
        output_gradient = contract_cols(shard_rows, out_weight).astype(jnp.bfloat16)
        grad_heads = jnp.transpose(
            output_gradient.reshape(tree_len, heads_local, HEAD_SIZE), (1, 0, 2)
        )
        totals_heads = log_totals.reshape(heads_local, tree_len)

        def one_head(head_id, carry):
            key_acc, value_acc, query_grad = carry
            kv_id = head_id // queries_per_group
            keys_all = lax.dynamic_index_in_dim(lookup_matrix, kv_id, axis=1, keepdims=False)
            values_all = lax.dynamic_index_in_dim(value_rows, kv_id, axis=1, keepdims=False)
            query_all = lax.dynamic_index_in_dim(asking_heads, head_id, axis=0, keepdims=False)
            grad_all = lax.dynamic_index_in_dim(grad_heads, head_id, axis=0, keepdims=False)
            own_all = lax.dynamic_index_in_dim(attended_heads, head_id, axis=0, keepdims=False)
            totals_all = lax.dynamic_index_in_dim(totals_heads, head_id, axis=0, keepdims=False)
            key_now = lax.dynamic_index_in_dim(key_acc, kv_id, axis=1, keepdims=False)
            value_now = lax.dynamic_index_in_dim(value_acc, kv_id, axis=1, keepdims=False)
            query_blocks = []
            for block_id in range(block_total):
                opening_slot = block_id * block_len
                closing_slot = opening_slot + block_len
                query_now = query_all[opening_slot:closing_slot]
                keys_now = keys_all[:closing_slot]
                values_now = values_all[:closing_slot]
                line_multiplier = softness_multiplier[opening_slot:closing_slot][:, None]
                attention_logits = jnp.where(
                    masks[block_id], contract_cols(query_now, keys_now) * line_multiplier, -jnp.inf
                )
                attention_probabilities = jnp.exp(
                    attention_logits - totals_all[opening_slot:closing_slot][:, None]
                )
                grad_rows = grad_all[opening_slot:closing_slot]
                own_rows = own_all[opening_slot:closing_slot]
                probability_cotangent = contract_cols(grad_rows, values_now)
                middle_point = jnp.sum(
                    grad_rows.astype(jnp.float32) * own_rows.astype(jnp.float32), axis=1
                )
                logit_cotangent = (
                    attention_probabilities
                    * (probability_cotangent - middle_point[:, None])
                    * line_multiplier
                ).astype(jnp.bfloat16)
                query_blocks.append(
                    jnp.dot(logit_cotangent, keys_now, preferred_element_type=jnp.float32).astype(
                        jnp.bfloat16
                    )
                )
                key_now = key_now.at[:closing_slot].add(contract_rows(logit_cotangent, query_now))
                value_now = value_now.at[:closing_slot].add(
                    contract_rows(attention_probabilities.astype(jnp.bfloat16), grad_rows)
                )
            key_acc = lax.dynamic_update_index_in_dim(key_acc, key_now, kv_id, axis=1)
            value_acc = lax.dynamic_update_index_in_dim(value_acc, value_now, kv_id, axis=1)
            query_grad = lax.dynamic_update_index_in_dim(
                query_grad, jnp.concatenate(query_blocks, axis=0), head_id, axis=0
            )
            return (key_acc, value_acc, query_grad)

        key_acc, value_acc, query_grad = lax.fori_loop(
            0,
            heads_local,
            one_head,
            (
                jnp.zeros((tree_len, kv_local, HEAD_SIZE), jnp.float32),
                jnp.zeros((tree_len, kv_local, HEAD_SIZE), jnp.float32),
                jnp.zeros((heads_local, tree_len, HEAD_SIZE), jnp.bfloat16),
            ),
        )
        query_grad = jnp.transpose(query_grad, (1, 0, 2)).reshape(
            tree_len, kv_local, queries_per_group, HEAD_SIZE
        )
        gradients = jnp.concatenate(
            [
                query_grad,
                key_acc.astype(jnp.bfloat16)[:, :, None],
                value_acc.astype(jnp.bfloat16)[:, :, None],
            ],
            axis=2,
        )
        gradients = gradients.reshape(tree_len, kv_local * (queries_per_group + 2) * HEAD_SIZE)
        return gradients

    def no_part():
        return jnp.zeros((tree_len, kv_local * (queries_per_group + 2) * HEAD_SIZE), jnp.bfloat16)

    gradients = lax.cond(lax.axis_index("ctx") >= 0, backward_part, no_part)
    returned = lax.all_to_all(gradients, "ctx", split_axis=0, concat_axis=1, tiled=True)
    return (returned, weight_total)


def solution(mesh):
    placed = (
        P(("leaf", "ctx"), None),
        P(("leaf", "ctx"), None),
        P("ctx", None),
        P("leaf", None),
        P("leaf"),
    )
    return jax.shard_map(
        local,
        mesh=mesh,
        in_specs=placed,
        out_specs=(P(("leaf", "ctx"), None), P("ctx", None)),
        check_vma=False,
    )
```

profile of v0, /device:TPU:1, one launch (start us, length us, event | category | flops | bytes accessed | tf_op | source)
XLA Modules:
  0.0 235.3 jit_solution(3943057925726047068)
XLA Ops:
  7.9 3.9 %copy.59 = bf16[128,7168]{0,1:T(8,128)(2,1)} copy(bf16[128,7168]{1,0:T(8,128)(2,1)} %param.23) | data formatting | bytes 3670016 | tf_op args[0]
  11.8 5.9 %all-to-all-start = ((bf16[128,8,896]{0,2,1:T(8,128)(2,1)}), bf16[128,8,896]{0,2,1:T(8,128)(2,1)S(1)}, u32[]{:S(2)}, u32[]{:S(2)}) async-start(bf16[128,8,896]{0,2,1:T(8,128)(2,1)} %bitcast.310), calls=%async_computation | async-start | bytes 3670016 | tf_op jit(solution)/shard_map/all_to_all | solution.py:57
  17.7 2.2 while.53
  26.5 27.9 %all-to-all-done = bf16[128,8,896]{0,2,1:T(8,128)(2,1)S(1)} async-done(((bf16[128,8,896]{0,2,1:T(8,128)(2,1)}), bf16[128,8,896]{0,2,1:T(8,128)(2,1)S(1)}, u32[]{:S(2)}, u32[]{:S(2)}) %all-to-all-start) | async-done | bytes 1835040 | tf_op jit(solution)/shard_map/all_to_all | solution.py:57
  54.4 2.4 %copy.60 = bf16[8,128,896]{1,0,2:T(8,128)(2,1)} copy(bf16[8,128,896]{1,2,0:T(8,128)(2,1)S(1)} %bitcast.309) | data formatting | bytes 3670016 | tf_op jit(solution)/shard_map/all_to_all | solution.py:57
  56.8 2.9 %reshape.557 = bf16[1024,1,7,128]{0,3,2,1:T(8,128)(2,1)S(1)} reshape(bf16[8,128,896]{1,0,2:T(8,128)(2,1)} %copy.60) | data formatting | bytes 3670016 | tf_op jit(solution)/shard_map/reshape | solution.py:61
  64.0 1.8 fusion.34
  65.8 2.2 exponential_reduce_fusion
  68.0 1.9 fusion.55
  69.9 3.7 %fusion.52 = bf16[512,1,5,128]{3,0,2,1:T(8,128)(2,1)S(1)} fusion(f32[1024,512,5]{1,0,2:T(8,128)S(1)} %get-tuple-element.624, f32[5,512]{1,0:T(8,128)S(1)} %log_add_fusion, f32[512]{0:T(512)S(1)} %get-tuple-element.622, pred[512,1024]{0,1:T(8,128)(4,1)S(1)} %copy-done.1, bf16[1024,1,7,128]{0,3,2,1:T(8,128)(2,1)S(1)} %reshape.557), kind=kOutput, calls=%fused_computation.85 | convolution fusion | flops 681902080 | bytes 11945984 | tf_op jit(solution)/shard_map/gjts,sgd->tgjd/dot_general | solution.py:94
  73.6 1.9 fusion.77
  75.5 2.5 %copy.70 = bf16[1024,1,5,128]{0,3,2,1:T(8,128)(2,1)} copy(bf16[1024,1,5,128]{3,0,2,1:T(8,128)(2,1)} %get-tuple-element.620) | data formatting | bytes 2621440 | tf_op jit(solution)/shard_map/concatenate | solution.py:102
  79.1 6.5 %all-gather.2.cloned.1.call-done = bf16[1024,5120]{1,0:T(8,128)(2,1)} async-done(((bf16[128,5120]{1,0:T(8,128)(2,1)}), bf16[1024,5120]{1,0:T(8,128)(2,1)}) %all-gather.2.cloned.1.call-update) | async-done | bytes 10485776 | tf_op jit(solution)/shard_map/all_gather | solution.py:105
  85.6 11.7 %convolution_convert_fusion.3 = bf16[640,5120]{1,0:T(8,128)(2,1)} fusion(bf16[1024,640]{0,1:T(8,128)(2,1)} %bitcast.316, bf16[1024,5120]{1,0:T(8,128)(2,1)} %all-gather.2.cloned.1.call-done), kind=kOutput, calls=%fused_computation.66 | convolution fusion | flops 6714163200 | bytes 18350080 | tf_op jit(solution)/shard_map/dot_general | solution.py:44
  97.4 85.4 %conditional.1 = (bf16[1024,896]{0,1:T(8,128)(2,1)S(1)}) conditional(s32[]{:T(128)} %convert_element_type.154, () %tuple.93, (bf16[1024,5120]{1,0:T(8,128)(2,1)}, bf16[640,5120]{1,0:T(8,128)(2,1)}, f32[1,5,1024]{2,1,0:T(8,128)S(1)}, bf16[5,1024,128]{1,2,0:T(8,128)(2,1)}, bf16[1024,1,128]{2,0,1:T(8,128)(2,1)S(1)}, /*index=5*/f32[1024]{0:T(1024)S(1)}, ...), branch_computations={%region_7.8_spmd, %region_8.13_spmd} | conditional | flops 7727873024 | bytes 52072836 | solution.py:218
  97.4 11.6 %convolution_convert_fusion.2 = bf16[1024,640]{0,1:T(8,128)(2,1)S(1)} fusion(bf16[1024,5120]{1,0:T(8,128)(2,1)} %get-tuple-element.479, bf16[640,5120]{1,0:T(8,128)(2,1)} %get-tuple-element.510), kind=kOutput, calls=%fused_computation.54 | convolution fusion | flops 6711541760 | bytes 18350080 | tf_op jit(solution)/shard_map/cond/branch_1_fun/dot_general | solution.py:50
  110.5 70.4 %while.52 = (s32[]{:T(128)}, f32[1024,1,128]{2,0,1:T(8,128)S(1)}, f32[1024,1,128]{2,0,1:T(8,128)S(1)}, bf16[5,1024,128]{1,2,0:T(8,128)(2,1)}, bf16[5,1024,128]{1...) while((s32[]{:T(128)}, f32[1024,1,128]{2,0,1:T(8,128)S(1)}, ...), condition=%wide.region_12.12_spmd, body=%wide.region_9.11_spmd.sunk | while | flops 1014496256 | bytes 24809708 | solution.py:191
  117.5 1.6 subtract_exponential_fusion.2
  184.0 3.1 %copy.72 = bf16[1024,896]{1,0:T(8,128)(2,1)S(1)} copy(bf16[1024,896]{0,1:T(8,128)(2,1)} %copy-done) | data formatting | bytes 3670016 | tf_op jit(solution)/shard_map/cond | solution.py:218
  187.0 27.0 %all_to_all.35 = bf16[8,128,896]{2,1,0:T(8,128)(2,1)} all-to-all(bf16[8,128,896]{2,1,0:T(8,128)(2,1)S(1)} %bitcast.311), channel_id=1, replica_groups=mesh['leaf'=16,'ctx'=8] {'ctx'}, dimensions={0} | all-to-all | bytes 3670016 | tf_op jit(solution)/shard_map/all_to_all | solution.py:219
  214.0 3.2 %copy.73 = bf16[8,128,896]{1,2,0:T(8,128)(2,1)S(1)} copy(bf16[8,128,896]{2,1,0:T(8,128)(2,1)} %all_to_all.35) | data formatting | bytes 3670016 | tf_op jit(solution)/shard_map/all_to_all | solution.py:219
  217.2 2.9 %copy.74 = bf16[128,7168]{1,0:T(8,128)(2,1)} copy(bf16[128,7168]{0,1:T(8,128)(2,1)S(1)} %bitcast.312) | data formatting | bytes 3670016
  220.1 2.3 all-reduce.2.cloned.1.call-done
  222.4 6.1 %copy.127 = bf16[640,5120]{1,0:T(8,128)(2,1)} copy(bf16[640,5120]{1,0:T(8,128)(2,1)} %all-reduce.2.cloned.1.call-done) | data formatting | bytes 13107200
  (158 shorter events, 87.6 us)
Async XLA Ops:
  7.2 78.5 %all-gather.2.cloned.1.call-start = ((), (), s32[]{:S(2)}) async-start(), calls=%async_computation.2 | async-start | bytes 11796480 | tf_op jit(solution)/shard_map/all_gather | solution.py:105
  11.8 6.0 %copy-start.3 = (s32[1,8]{1,0:T(1,128)S(1)}, s32[1,8]{1,0:T(1,128)}, u32[]{:S(2)}) copy-start(s32[1,8]{1,0:T(1,128)} %param.26) | copy-start | bytes 100
  11.8 42.6 %all-to-all-start = ((bf16[128,8,896]{0,2,1:T(8,128)(2,1)}), bf16[128,8,896]{0,2,1:T(8,128)(2,1)S(1)}, u32[]{:S(2)}, u32[]{:S(2)}) async-start(bf16[128,8,896]{0,2,1:T(8,128)(2,1)} %bitcast.310), calls=%async_computation | async-start | bytes 3670016 | tf_op jit(solution)/shard_map/all_to_all | solution.py:57
  17.7 204.7 %all-reduce.2.cloned.1.call-start = ((), (), s32[]{:S(2)}) async-start(), calls=%async_computation.3 | async-start | bytes 13107200 | tf_op jit(solution)/shard_map/psum | solution.py:130
  20.0 6.5 %copy-start.2 = (s32[1024]{0:T(1024)S(1)}, s32[1024]{0:T(1024)}, u32[]{:S(2)}) copy-start(s32[1024]{0:T(1024)} %param.27) | copy-start | bytes 12292
  62.8 1.2 copy-start.1
  182.7 1.2 copy-start
Sparse Core Ops, SparseCore 0:
  9.7 75.9 all-gather.1
  97.5 124.8 all-reduce.1
where the time goes:
time: 237 us; the launch traced here: 235 us
  matrix products  89.8 us (38%)
  local copies, waits for them, and re-layouts  43.5 us (18%)
  waiting for transfers between devices  37.4 us (16%)
  blocking collectives  27 us (11%)
  other arithmetic  16.8 us (7%)
  between operations  14.2 us (6%)
  starting transfers between devices  5.97 us (3%)
    dot_general x21, matrix products, contract_cols(): lax.dot_general(left, right, (((1,), (1,)), ((), ())), preferred_element_...  39.5 us
    dot_general x21, matrix products, contract_rows(): lax.dot_general(left, right, (((0,), (0,)), ((), ())), preferred_element_...  38.2 us
    all_to_all x1, waiting for transfers between devices, local(): lax.all_to_all(query_key_value_rows, 'ctx', split_axis=1, concat_axis=0,...  27.9 us
    all_to_all x1, blocking collectives, local(): lax.all_to_all(gradients, 'ctx', split_axis=0, concat_axis=1, tiled=True)  27 us
    unnamed x13, local copies, waits for them, and re-layouts  15.4 us
    reduce_sum x5, other arithmetic, one_head(): jnp.sum(grad_rows.astype(jnp.float32) * own_rows.astype(jnp.float32), axi...  6.59 us
    all_gather x1, waiting for transfers between devices, local(): shard_rows = lax.all_gather(cotangent, 'ctx', axis=0, tiled=True)  6.48 us
    all_to_all x1, starting transfers between devices, local(): lax.all_to_all(query_key_value_rows, 'ctx', split_axis=1, concat_axis=0,...  5.93 us
  transfers between devices with their start and end apart: 3, of which 3 were waited for; matrix products, arithmetic and copies ran while one was open for 56% of the time, Pallas kernels for 0%

commit v1 on v0

--- a/solution.py
+++ b/solution.py
@@ -1,3 +1,4 @@
+import functools
 import math
 import jax
 import jax.numpy as jnp
@@ -9,6 +10,19 @@
 HEAD_SIZE = 128
 BLK = 128
 log_base = 1024.0
+
+
+def supply_all_the_stages_all(original, across, dim_at):
+    all_rows = jnp.concatenate(
+        lax.all_to_all(
+            jnp.stack(tuple((original for _ in range(lax.axis_size(across))))), across, 0, 0
+        ),
+        dim_at,
+    )
+    return all_rows
+
+
+get_samples_for = functools.partial(supply_all_the_stages_all, across="ctx", dim_at=0)
 
 
 def ancestors(parents):
@@ -102,7 +116,7 @@
     attended = jnp.concatenate(attended_parts, axis=0)
     log_totals = jnp.concatenate(total_parts, axis=2)
     flat_out = attended.reshape(tree_len, heads_local * HEAD_SIZE)
-    shard_rows = lax.all_gather(cotangent, "ctx", axis=0, tiled=True)
+    shard_rows = get_samples_for(cotangent)
     weight_low = contract_rows(flat_out, shard_rows).astype(jnp.bfloat16)
     asking_heads = jnp.transpose(asking_matrix.reshape(tree_len, heads_local, HEAD_SIZE), (1, 0, 2))
     attended_heads = jnp.transpose(attended.reshape(tree_len, heads_local, HEAD_SIZE), (1, 0, 2))

time: 237 us -> 320 us (1.35)
  waiting for transfers between devices: 37.4 us -> 84.4 us
  blocking collectives: 27 us -> 57.2 us
  local copies, waits for them, and re-layouts: 43.5 us -> 49.9 us
    all_to_all x1, waiting for transfers between devices: 27.9 us -> 82.8 us  [supply_all_the_stages_all(): lax.all_to_all(jnp.stack(tuple((original for _ in range(lax.axis_size(acr...]
    all_to_all x0 -> x1, blocking collectives: none -> 29.6 us  [local(): lax.all_to_all(query_key_value_rows, 'ctx', split_axis=1, concat_axis=0,...]
    all_gather x1 -> x0, waiting for transfers between devices: 6.48 us -> none  [local(): shard_rows = lax.all_gather(cotangent, 'ctx', axis=0, tiled=True)]
    another operation x2 -> x3, local copies, waits for them, and re-layouts: 0.07 us -> 5.33 us  [the longest x1 5.26 us: supply_all_the_stages_all(): jnp.stack(tuple((original for _ in range(lax.axis_size(across)))))]
    unnamed x13 -> x15, local copies, waits for them, and re-layouts: 15.4 us -> 15.4 us
  transfers between devices with their start and end apart: 3 -> 2, of which waited for: 3 -> 2; matrix products, arithmetic and copies ran while one was open for 56% -> 40% of each run, Pallas kernels for 0% -> 0%
where the time goes in v1:
time: 320 us; the launch traced here: 319 us
  matrix products  89.8 us (28%)
  waiting for transfers between devices  84.4 us (26%)
  blocking collectives  57.2 us (18%)
  local copies, waits for them, and re-layouts  49.9 us (16%)
  other arithmetic  16.4 us (5%)
  between operations  14.2 us (4%)
  starting transfers between devices  6.2 us (2%)
    all_to_all x1, waiting for transfers between devices, supply_all_the_stages_all(): lax.all_to_all(jnp.stack(tuple((original for _ in range(lax.axis_size(acr...  82.8 us
    dot_general x21, matrix products, contract_cols(): lax.dot_general(left, right, (((1,), (1,)), ((), ())), preferred_element_...  39.6 us
    dot_general x21, matrix products, contract_rows(): lax.dot_general(left, right, (((0,), (0,)), ((), ())), preferred_element_...  38.2 us
    all_to_all x1, blocking collectives, local(): lax.all_to_all(query_key_value_rows, 'ctx', split_axis=1, concat_axis=0,...  29.6 us
    all_to_all x1, blocking collectives, local(): lax.all_to_all(gradients, 'ctx', split_axis=0, concat_axis=1, tiled=True)  27.6 us
    unnamed x15, local copies, waits for them, and re-layouts  15.4 us
    reduce_sum x5, other arithmetic, one_head(): jnp.sum(grad_rows.astype(jnp.float32) * own_rows.astype(jnp.float32), axi...  6.56 us
  transfers between devices with their start and end apart: 2, of which 2 were waited for; matrix products, arithmetic and copies ran while one was open for 40% of the time, Pallas kernels for 0%

profile of v1, /device:TPU:1, one launch (start us, length us, event | category | flops | bytes accessed | tf_op | source)
XLA Modules:
  0.0 318.7 jit_solution(4310144309406683412)
XLA Ops:
  7.2 3.9 %copy.59 = bf16[128,7168]{0,1:T(8,128)(2,1)} copy(bf16[128,7168]{1,0:T(8,128)(2,1)} %param.23) | data formatting | bytes 3670016 | tf_op args[0]
  11.0 29.6 %all_to_all.40 = bf16[128,8,896]{0,2,1:T(8,128)(2,1)S(1)} all-to-all(bf16[128,8,896]{0,2,1:T(8,128)(2,1)} %bitcast.313), channel_id=1, replica_groups=mesh['leaf'=16,'ctx'=8] {'ctx'}, dimensions={1} | all-to-all | bytes 3670016 | tf_op jit(solution)/shard_map/all_to_all | solution.py:71
  40.6 5.3 %stack.2 = bf16[8,128,5120]{2,1,0:T(8,128)(2,1)} broadcast(bf16[128,5120]{1,0:T(8,128)(2,1)S(1)} %copy-done.3), dimensions={1,2} | broadcast | bytes 11796480 | tf_op jit(solution)/shard_map/stack | solution.py:18
  45.9 6.2 %all-to-all-start.1 = ((bf16[8,128,5120]{2,1,0:T(8,128)(2,1)}), bf16[8,128,5120]{2,1,0:T(8,128)(2,1)}, u32[]{:S(2)}, u32[]{:S(2)}) async-start(bf16[8,128,5120]{2,1,0:T(8,128)(2,1)} %stack.2), calls=%async_computation.1 | async-start | bytes 20971520 | tf_op jit(solution)/shard_map/all_to_all | solution.py:17
  52.1 2.2 while.53
  60.8 2.4 copy.60
  63.2 2.9 reshape.562
  70.3 1.8 fusion.34
  72.2 2.2 exponential_reduce_fusion
  74.4 1.9 fusion.55
  76.3 3.7 %fusion.52 = bf16[512,1,5,128]{3,0,2,1:T(8,128)(2,1)S(1)} fusion(f32[1024,512,5]{1,0,2:T(8,128)S(1)} %get-tuple-element.624, f32[5,512]{1,0:T(8,128)S(1)} %log_add_fusion, f32[512]{0:T(512)S(1)} %get-tuple-element.622, pred[512,1024]{0,1:T(8,128)(4,1)S(1)} %copy-done.1, bf16[1024,1,7,128]{0,3,2,1:T(8,128)(2,1)S(1)} %reshape.562), kind=kOutput, calls=%fused_computation.85 | convolution fusion | flops 681902080 | bytes 11945984 | tf_op jit(solution)/shard_map/gjts,sgd->tgjd/dot_general | solution.py:108
  80.0 1.9 fusion.77
  81.9 2.5 copy.70
  85.6 82.8 %all-to-all-done.1 = bf16[8,128,5120]{2,1,0:T(8,128)(2,1)} async-done(((bf16[8,128,5120]{2,1,0:T(8,128)(2,1)}), bf16[8,128,5120]{2,1,0:T(8,128)(2,1)}, u32[]{:S(2)}, u32[]{:S(2)}) %all-to-all-start.1) | async-done | bytes 10485792 | tf_op jit(solution)/shard_map/all_to_all | solution.py:17
  168.4 11.7 %convolution_convert_fusion.3 = bf16[640,5120]{1,0:T(8,128)(2,1)} fusion(bf16[1024,640]{0,1:T(8,128)(2,1)} %bitcast.317, bf16[1024,5120]{1,0:T(8,128)(2,1)} %bitcast.54), kind=kOutput, calls=%fused_computation.66 | convolution fusion | flops 6714163200 | bytes 18350080 | tf_op jit(solution)/shard_map/dot_general | solution.py:58
  180.1 86.2 %conditional.1 = (bf16[1024,896]{0,1:T(8,128)(2,1)S(1)}) conditional(s32[]{:T(128)} %convert_element_type.154, () %tuple.93, (bf16[1024,5120]{1,0:T(8,128)(2,1)}, bf16[640,5120]{1,0:T(8,128)(2,1)}, f32[1,5,1024]{2,1,0:T(8,128)S(1)}, bf16[5,1024,128]{1,2,0:T(8,128)(2,1)}, bf16[1024,1,128]{2,0,1:T(8,128)(2,1)S(1)}, /*index=5*/f32[1024]{0:T(1024)S(1)}, ...), branch_computations={%region_7.8_spmd, %region_8.13_spmd} | conditional | flops 7727873024 | bytes 57315744 | solution.py:232
  180.1 11.6 %convolution_convert_fusion.2 = bf16[1024,640]{0,1:T(8,128)(2,1)S(1)} fusion(bf16[1024,5120]{1,0:T(8,128)(2,1)} %get-tuple-element.479, bf16[640,5120]{1,0:T(8,128)(2,1)} %get-tuple-element.510), kind=kOutput, calls=%fused_computation.54 | convolution fusion | flops 6711541760 | bytes 18350080 | tf_op jit(solution)/shard_map/cond/branch_1_fun/dot_general | solution.py:64
  193.3 70.4 %while.52 = (s32[]{:T(128)}, f32[1024,1,128]{2,0,1:T(8,128)S(1)}, f32[1024,1,128]{2,0,1:T(8,128)S(1)}, bf16[5,1024,128]{1,2,0:T(8,128)(2,1)}, bf16[5,1024,128]{1...) while((s32[]{:T(128)}, f32[1024,1,128]{2,0,1:T(8,128)S(1)}, ...), condition=%wide.region_12.12_spmd, body=%wide.region_9.11_spmd.sunk | while | flops 1014496256 | bytes 24809708 | solution.py:205
  228.4 1.6 subtract_exponential_fusion.2
  267.5 3.1 copy.72
  270.6 27.6 %all_to_all.41 = bf16[8,128,896]{2,1,0:T(8,128)(2,1)} all-to-all(bf16[8,128,896]{2,1,0:T(8,128)(2,1)S(1)} %bitcast.311), channel_id=1, replica_groups=mesh['leaf'=16,'ctx'=8] {'ctx'}, dimensions={0} | all-to-all | bytes 3670016 | tf_op jit(solution)/shard_map/all_to_all | solution.py:233
  298.2 3.2 copy.73
  301.4 2.9 copy.74
  305.8 6.1 %copy.127 = bf16[640,5120]{1,0:T(8,128)(2,1)} copy(bf16[640,5120]{1,0:T(8,128)(2,1)} %all-reduce.2.cloned.1.call-done) | data formatting | bytes 13107200
  (161 shorter events, 89.1 us)
Async XLA Ops:
  11.0 29.6 %copy-start.3 = (bf16[128,5120]{1,0:T(8,128)(2,1)S(1)}, bf16[128,5120]{1,0:T(8,128)(2,1)}, u32[]{:S(2)}) copy-start(bf16[128,5120]{1,0:T(8,128)(2,1)} %param.24) | copy-start | bytes 3932164
  45.9 6.2 %copy-start.5 = (s32[1,8]{1,0:T(1,128)S(1)}, s32[1,8]{1,0:T(1,128)}, u32[]{:S(2)}) copy-start(s32[1,8]{1,0:T(1,128)} %param.26) | copy-start | bytes 100
  45.9 122.5 %all-to-all-start.1 = ((bf16[8,128,5120]{2,1,0:T(8,128)(2,1)}), bf16[8,128,5120]{2,1,0:T(8,128)(2,1)}, u32[]{:S(2)}, u32[]{:S(2)}) async-start(bf16[8,128,5120]{2,1,0:T(8,128)(2,1)} %stack.2), calls=%async_computation.1 | async-start | bytes 20971520 | tf_op jit(solution)/shard_map/all_to_all | solution.py:17
  52.1 253.7 %all-reduce.2.cloned.1.call-start = ((), (), s32[]{:S(2)}) async-start(), calls=%async_computation.3 | async-start | bytes 13107200 | tf_op jit(solution)/shard_map/psum | solution.py:144
  54.3 6.5 %copy-start.4 = (s32[1024]{0:T(1024)S(1)}, s32[1024]{0:T(1024)}, u32[]{:S(2)}) copy-start(s32[1024]{0:T(1024)} %param.27) | copy-start | bytes 12292
  69.2 1.1 copy-start.1
  263.7 1.4 copy-start.2
  266.3 1.2 copy-start
Sparse Core Ops, SparseCore 0:
  180.2 125.4 all-reduce.1
